TPU v7x, 256 devices: a whole 4x4x8 slice. The times are simulated.
256 devices in a mesh: row: 8 (over z), col: 32 (over y, x, core).
Axes of the slice: x: 4, y: 4, z: 8, core: 2. Of those that a mesh axis runs over, the one named last changes fastest.
Arguments:
- embeds: bfloat16 [24576, 768], P('col'), may hold values from -6 to 6
- labels: bfloat16 [24576, 1000], P('col'), may hold values from -6 to 6
- sharpness: float32 [24576], P('col'), may hold values from 0.5 to 100
- pattern: int32 [192, 16], P('col'), may hold values from 0 to 191, as said below
- mask_pos: int32 [24576, 50], P('col'), may hold values from 0 to 2047, as said below
Outputs:
- propagated: bfloat16 [24576, 1000], P('col', 'row')
Inputs may be any that keep to these rules, and one draw needn't show every extreme that they name: `pattern`: split the row blocks into runs of 6 and the slots into runs of 2; within one run of row blocks and one run of slots, ids that lie in the same run of 6 block ids are equal. `mask_pos`: the 50 positions of a row are distinct; position k * 128 + m names row m of the row block's k-th candidate block.
All inputs are finite; a program needn't handle non-finite values.
Results may differ from a plain program's by a relative error of at most 0.012.
Values may be sent and summed in bfloat16 or wider, within the bound.
No kernel may reach another device: no remote copies, remote signals or barrier semaphores. Data moves between devices by JAX's collectives and lax.ppermute only.
A program may use at most 128 MiB of HBM per device.

v0:
```python
import math
import jax
import jax.numpy as jnp
from jax import lax
from jax.sharding import PartitionSpec as P

BLOCK = 128
SLOTS = 16
CHUNKS = 4
mixing = 0.75
lowest_logit = -1e30


def body(embeds, labels, sharpness, pattern, mask_pos):
    rows_here, width = embeds.shape
    classes = labels.shape[1]
    n_col = lax.axis_size("col")
    n_row = lax.axis_size("row")
    row_pos = lax.axis_index("row")
    blocks_here = rows_here // BLOCK
    slots_here = SLOTS // n_row
    span = slots_here * BLOCK
    my_slots = lax.dynamic_slice_in_dim(pattern, row_pos * slots_here, slots_here, 1)
    owners = my_slots // blocks_here
    local_ids = my_slots % blocks_here
    peers = jnp.arange(n_col, dtype=jnp.int32)
    wanted = jnp.max(jnp.where(owners[..., None] == peers, local_ids[..., None], 0), axis=(0, 1))
    requested = lax.all_to_all(wanted, "col", split_axis=0, concat_axis=0, tiled=True)
    embedding_tiles = embeds.reshape(blocks_here, BLOCK, width)
    send_emb = embedding_tiles[requested]
    shifted = mask_pos - row_pos * span
    shifted = jnp.where((shifted >= 0) & (shifted < span), shifted, span)
    positions = jnp.arange(span, dtype=jnp.int32)
    in_mask = jnp.any(shifted[:, :, None] == positions[None, None, :], axis=1)
    in_mask = in_mask.reshape(blocks_here, BLOCK, span)

    def propagate_using(weight_matrix, fetched_lab):
        width_here = fetched_lab.shape[-1]
        candidate_ids = fetched_lab[owners].reshape(blocks_here, span, width_here)
        blended_rows = jnp.einsum(
            "tmg,tgh->tmh", weight_matrix, candidate_ids, preferred_element_type=jnp.float32
        )
        return blended_rows.reshape(rows_here, width_here)

    fetched_emb = lax.all_to_all(send_emb, "col", split_axis=0, concat_axis=0, tiled=True)
    candidate_ids = fetched_emb[owners].reshape(blocks_here, span, width)
    scores = jnp.einsum(
        "evg,erg->evr", embedding_tiles, candidate_ids, preferred_element_type=jnp.float32
    ) / math.sqrt(width)
    logits = scores * sharpness.reshape(blocks_here, BLOCK, 1)
    local_max = jnp.max(jnp.where(in_mask, logits, lowest_logit), axis=2)
    local_sum = jnp.sum(jnp.where(in_mask, jnp.exp(logits - local_max[..., None]), 0.0), axis=2)
    stats = lax.all_gather(jnp.stack([local_max, local_sum]), "row")
    top = jnp.max(stats[:, 0], axis=0)
    totals = jnp.sum(stats[:, 1] * jnp.exp(stats[:, 0] - top), axis=0)
    weight_matrix = jnp.where(
        in_mask, jnp.exp(logits - top[..., None]) / totals[..., None], 0.0
    ).astype(jnp.bfloat16)
    rows_dev = rows_here // n_row
    piece = classes // CHUNKS
    lab_chunks = labels.reshape(rows_here, CHUNKS, piece).transpose(1, 0, 2)
    fetched = []
    for k in range(CHUNKS):
        send_lab = lab_chunks[k].reshape(blocks_here, BLOCK, piece)[requested]
        fetched.append(lax.all_to_all(send_lab, "col", split_axis=0, concat_axis=0, tiled=True))
    sums = []
    for k in range(CHUNKS):
        partial_one = propagate_using(weight_matrix, fetched[k]).astype(jnp.bfloat16)
        if k > 0:
            partial_one, sums[k - 1] = lax.optimization_barrier((partial_one, sums[k - 1]))
        sums.append(lax.psum(partial_one, "row"))
    spreads = []
    for k in range(CHUNKS):
        summed = sums[k].astype(jnp.float32)
        spread = (mixing * summed + (1.0 - mixing) * lab_chunks[k].astype(jnp.float32)).astype(
            jnp.bfloat16
        )
        send_spread = spread.reshape(blocks_here, BLOCK, piece)[requested]
        spreads.append(lax.all_to_all(send_spread, "col", split_axis=0, concat_axis=0, tiled=True))
    shares = []
    for k in range(CHUNKS):
        partial_two = propagate_using(weight_matrix, spreads[k]).astype(jnp.bfloat16)
        if k > 0:
            partial_two, shares[k - 1] = lax.optimization_barrier((partial_two, shares[k - 1]))
        shares.append(lax.psum_scatter(partial_two, "row", scatter_dimension=0, tiled=True))
    outs = []
    for k in range(CHUNKS):
        seed_rows = lax.dynamic_slice_in_dim(lab_chunks[k], row_pos * rows_dev, rows_dev, 0)
        share = shares[k].astype(jnp.float32)
        outs.append(
            (mixing * share + (1.0 - mixing) * seed_rows.astype(jnp.float32)).astype(jnp.bfloat16)
        )
    mine = jnp.concatenate(outs, axis=1)
    return lax.all_to_all(mine, "row", split_axis=1, concat_axis=0, tiled=True)


def solution(mesh):
    placed = (P("col", None), P("col", None), P("col"), P("col", None), P("col", None))
    return jax.shard_map(
        body, mesh=mesh, in_specs=placed, out_specs=P("col", "row"), check_vma=False
    )
```

profile of v0, /device:TPU:4, one launch (start us, length us, event | category | flops | bytes accessed | tf_op | source)
XLA Modules:
  0.0 808.5 jit_solution(6084548880981616726)
XLA Ops:
  35.3 23.3 %all-to-all-done.4 = bf16[32,128,250]{2,1,0:T(8,128)(2,1)} async-done(((bf16[32,128,250]{2,1,0:T(8,128)(2,1)}), bf16[32,128,250]{2,1,0:T(8,128)(2,1)}, u32[]{:S(2)}, u32[]{:S(2)}) %all-to-all-start.4) | async-done | bytes 2048032 | tf_op jit(solution)/shard_map/all_to_all | solution.py:65
  58.6 8.4 %all-to-all-start.3 = ((bf16[32,128,250]{2,1,0:T(8,128)(2,1)}), bf16[32,128,250]{2,1,0:T(8,128)(2,1)}, u32[]{:S(2)}, u32[]{:S(2)}) async-start(bf16[32,128,250]{2,1,0:T(8,128)(2,1)} %gather_fusion.4), calls=%async_computation.3 | async-start | bytes 4194304 | tf_op jit(solution)/shard_map/all_to_all | solution.py:65
  70.6 22.9 %all-to-all-done.3 = bf16[32,128,250]{2,1,0:T(8,128)(2,1)} async-done(((bf16[32,128,250]{2,1,0:T(8,128)(2,1)}), bf16[32,128,250]{2,1,0:T(8,128)(2,1)}, u32[]{:S(2)}, u32[]{:S(2)}) %all-to-all-start.3) | async-done | bytes 2048032 | tf_op jit(solution)/shard_map/all_to_all | solution.py:65
  93.5 8.5 %all-to-all-start.1 = ((bf16[32,128,768]{2,1,0:T(8,128)(2,1)}), bf16[32,128,768]{2,1,0:T(8,128)(2,1)}, u32[]{:S(2)}, u32[]{:S(2)}) async-start(bf16[32,128,768]{2,1,0:T(8,128)(2,1)} %gather_fusion), calls=%async_computation.1 | async-start | bytes 12582912 | tf_op jit(solution)/shard_map/all_to_all | solution.py:45
  105.2 70.4 %all-to-all-done.1 = bf16[32,128,768]{2,1,0:T(8,128)(2,1)} async-done(((bf16[32,128,768]{2,1,0:T(8,128)(2,1)}), bf16[32,128,768]{2,1,0:T(8,128)(2,1)}, u32[]{:S(2)}, u32[]{:S(2)}) %all-to-all-start.1) | async-done | bytes 6291488 | tf_op jit(solution)/shard_map/all_to_all | solution.py:45
  175.5 9.1 %all-to-all-start.2 = ((bf16[32,128,250]{2,1,0:T(8,128)(2,1)}), bf16[32,128,250]{2,1,0:T(8,128)(2,1)}, u32[]{:S(2)}, u32[]{:S(2)}) async-start(bf16[32,128,250]{2,1,0:T(8,128)(2,1)} %gather_fusion.2), calls=%async_computation.2 | async-start | bytes 4194304 | tf_op jit(solution)/shard_map/all_to_all | solution.py:65
  203.4 7.8 all-to-all-done.2
  211.1 8.4 %all-to-all-start.7 = ((bf16[32,128,250]{2,1,0:T(8,128)(2,1)}), bf16[32,128,250]{2,1,0:T(8,128)(2,1)}, u32[]{:S(2)}, u32[]{:S(2)}) async-start(bf16[32,128,250]{2,1,0:T(8,128)(2,1)} %gather_fusion.12), calls=%async_computation.7 | async-start | bytes 4194304 | tf_op jit(solution)/shard_map/all_to_all | solution.py:65
  222.3 28.4 %all-gather = f32[16,6,128]{2,1,0:T(8,128)S(1)} all-gather(f32[2,6,128]{2,1,0:T(8,128)S(1)} %pad_maximum_fusion.1), channel_id=2, replica_groups=mesh['row'=8,'col'=32] {'row'}, dimensions={0}, use_global_device_ids=true | all-gather | bytes 55296 | tf_op jit(solution)/shard_map/all_gather | solution.py:53
  254.7 70.1 %all-reduce.5.cloned.1.call-done = bf16[768,250]{0,1:T(8,128)(2,1)} async-done(((bf16[768,250]{0,1:T(8,128)(2,1)}), bf16[768,250]{0,1:T(8,128)(2,1)}) %all-reduce.5.cloned.1.call-update) | async-done | bytes 384016 | tf_op jit(solution)/shard_map/psum | solution.py:71
  328.4 70.6 %all-reduce.7.cloned.1.call-done = bf16[768,250]{0,1:T(8,128)(2,1)} async-done(((bf16[768,250]{0,1:T(8,128)(2,1)}), bf16[768,250]{0,1:T(8,128)(2,1)}) %all-reduce.7.cloned.1.call-update) | async-done | bytes 384016 | tf_op jit(solution)/shard_map/psum | solution.py:71
  402.5 70.6 %all-reduce.9.cloned.1.call-done = bf16[768,250]{0,1:T(8,128)(2,1)} async-done(((bf16[768,250]{0,1:T(8,128)(2,1)}), bf16[768,250]{0,1:T(8,128)(2,1)}) %all-reduce.9.cloned.1.call-update) | async-done | bytes 384016 | tf_op jit(solution)/shard_map/psum | solution.py:71
  474.1 73.1 %all-reduce.11.cloned.1.call-done = bf16[768,250]{0,1:T(8,128)(2,1)} async-done(((bf16[768,250]{0,1:T(8,128)(2,1)}), bf16[768,250]{0,1:T(8,128)(2,1)}) %all-reduce.11.cloned.1.call-update) | async-done | bytes 384016 | tf_op jit(solution)/shard_map/psum | solution.py:71
  553.2 7.6 all-to-all-start.6
  563.0 24.2 %all-to-all-done.6 = bf16[32,128,250]{2,1,0:T(8,128)(2,1)} async-done(((bf16[32,128,250]{2,1,0:T(8,128)(2,1)}), bf16[32,128,250]{2,1,0:T(8,128)(2,1)}, u32[]{:S(2)}, u32[]{:S(2)}) %all-to-all-start.6) | async-done | bytes 2048032 | tf_op jit(solution)/shard_map/all_to_all | solution.py:79
  587.2 8.3 %all-to-all-start.5 = ((bf16[32,128,250]{2,1,0:T(8,128)(2,1)}), bf16[32,128,250]{2,1,0:T(8,128)(2,1)}, u32[]{:S(2)}, u32[]{:S(2)}) async-start(bf16[32,128,250]{2,1,0:T(8,128)(2,1)} %gather_fusion.8), calls=%async_computation.5 | async-start | bytes 4194304 | tf_op jit(solution)/shard_map/all_to_all | solution.py:79
  597.7 24.3 %all-to-all-done.5 = bf16[32,128,250]{2,1,0:T(8,128)(2,1)} async-done(((bf16[32,128,250]{2,1,0:T(8,128)(2,1)}), bf16[32,128,250]{2,1,0:T(8,128)(2,1)}, u32[]{:S(2)}, u32[]{:S(2)}) %all-to-all-start.5) | async-done | bytes 2048032 | tf_op jit(solution)/shard_map/all_to_all | solution.py:79
  622.0 8.4 %all-to-all-start.8 = ((bf16[32,128,250]{2,1,0:T(8,128)(2,1)}), bf16[32,128,250]{2,1,0:T(8,128)(2,1)}, u32[]{:S(2)}, u32[]{:S(2)}) async-start(bf16[32,128,250]{2,1,0:T(8,128)(2,1)} %gather_fusion.14), calls=%async_computation.8 | async-start | bytes 4194304 | tf_op jit(solution)/shard_map/all_to_all | solution.py:79
  635.9 20.9 %all-to-all-done.8 = bf16[32,128,250]{2,1,0:T(8,128)(2,1)} async-done(((bf16[32,128,250]{2,1,0:T(8,128)(2,1)}), bf16[32,128,250]{2,1,0:T(8,128)(2,1)}, u32[]{:S(2)}, u32[]{:S(2)}) %all-to-all-start.8) | async-done | bytes 2048032 | tf_op jit(solution)/shard_map/all_to_all | solution.py:79
  656.9 8.3 %all-to-all-start.9 = ((bf16[32,128,250]{2,1,0:T(8,128)(2,1)}), bf16[32,128,250]{2,1,0:T(8,128)(2,1)}, u32[]{:S(2)}, u32[]{:S(2)}) async-start(bf16[32,128,250]{2,1,0:T(8,128)(2,1)} %gather_fusion.16), calls=%async_computation.9 | async-start | bytes 4194304 | tf_op jit(solution)/shard_map/all_to_all | solution.py:79
  674.1 34.3 %reduce-scatter.15.cloned.1.call-done = bf16[96,250]{1,0:T(8,128)(2,1)} async-done(((bf16[768,250]{1,0:T(8,128)(2,1)}), bf16[96,250]{1,0:T(8,128)(2,1)}) %reduce-scatter.15.cloned.1.call-update) | async-done | bytes 48016
  712.6 34.4 %reduce-scatter.17.cloned.1.call-done = bf16[96,250]{1,0:T(8,128)(2,1)} async-done(((bf16[768,250]{1,0:T(8,128)(2,1)}), bf16[96,250]{1,0:T(8,128)(2,1)}) %reduce-scatter.17.cloned.1.call-update) | async-done | bytes 48016
  751.0 34.6 %reduce-scatter.19.cloned.1.call-done = bf16[96,250]{1,0:T(8,128)(2,1)} async-done(((bf16[768,250]{1,0:T(8,128)(2,1)}), bf16[96,250]{1,0:T(8,128)(2,1)}) %reduce-scatter.19.cloned.1.call-update) | async-done | bytes 48016
  787.0 14.0 %all_to_all.76 = bf16[96,8,125]{2,0,1:T(8,128)(2,1)S(1)} all-to-all(bf16[96,8,125]{2,0,1:T(8,128)(2,1)S(1)} %copy.203), channel_id=1, replica_groups=mesh['row'=8,'col'=32] {'row'}, dimensions={1} | all-to-all | bytes 384000 | tf_op jit(solution)/shard_map/all_to_all | solution.py:94
  (111 shorter events, 103.6 us)
Async XLA Ops:
  6.5 60.5 %copy-start = (bf16[768,768]{1,0:T(8,128)(2,1)S(1)}, bf16[768,768]{1,0:T(8,128)(2,1)}, u32[]{:S(2)}) copy-start(bf16[768,768]{1,0:T(8,128)(2,1)} %param.5) | copy-start | bytes 3538948
  8.8 12.8 %all-to-all-start = ((s32[32,1,1]{2,1,0:T(1,128)}), s32[32,1,1]{2,1,0:T(1,128)S(1)}, u32[]{:S(2)}, u32[]{:S(2)}) async-start(s32[32,1,1]{2,1,0:T(1,128)} %copy.173), calls=%async_computation | async-start | bytes 32768 | tf_op jit(solution)/shard_map/all_to_all | solution.py:28
  25.4 33.2 %all-to-all-start.4 = ((bf16[32,128,250]{2,1,0:T(8,128)(2,1)}), bf16[32,128,250]{2,1,0:T(8,128)(2,1)}, u32[]{:S(2)}, u32[]{:S(2)}) async-start(bf16[32,128,250]{2,1,0:T(8,128)(2,1)} %gather_fusion.6), calls=%async_computation.4 | async-start | bytes 4194304 | tf_op jit(solution)/shard_map/all_to_all | solution.py:65
  58.6 34.9 %all-to-all-start.3 = ((bf16[32,128,250]{2,1,0:T(8,128)(2,1)}), bf16[32,128,250]{2,1,0:T(8,128)(2,1)}, u32[]{:S(2)}, u32[]{:S(2)}) async-start(bf16[32,128,250]{2,1,0:T(8,128)(2,1)} %gather_fusion.4), calls=%async_computation.3 | async-start | bytes 4194304 | tf_op jit(solution)/shard_map/all_to_all | solution.py:65
  93.5 82.0 %all-to-all-start.1 = ((bf16[32,128,768]{2,1,0:T(8,128)(2,1)}), bf16[32,128,768]{2,1,0:T(8,128)(2,1)}, u32[]{:S(2)}, u32[]{:S(2)}) async-start(bf16[32,128,768]{2,1,0:T(8,128)(2,1)} %gather_fusion), calls=%async_computation.1 | async-start | bytes 12582912 | tf_op jit(solution)/shard_map/all_to_all | solution.py:45
  105.2 79.5 %copy-start.7 = (s32[6,2]{1,0:T(8,128)S(1)}, s32[6,2]{1,0:T(8,128)}, u32[]{:S(2)}) copy-start(s32[6,2]{1,0:T(8,128)} %get-tuple-element.29) | copy-start | bytes 148
  105.2 79.6 %copy-start.6 = (s32[768,50]{0,1:T(8,128)S(1)}, s32[768,50]{0,1:T(8,128)}, u32[]{:S(2)}) copy-start(s32[768,50]{0,1:T(8,128)} %param.9) | copy-start | bytes 460804
  105.2 88.0 %copy-start.8 = (f32[768]{0:T(1024)S(1)}, f32[768]{0:T(1024)}, u32[]{:S(2)}) copy-start(f32[768]{0:T(1024)} %param.7) | copy-start | bytes 9220
  175.5 35.6 %all-to-all-start.2 = ((bf16[32,128,250]{2,1,0:T(8,128)(2,1)}), bf16[32,128,250]{2,1,0:T(8,128)(2,1)}, u32[]{:S(2)}, u32[]{:S(2)}) async-start(bf16[32,128,250]{2,1,0:T(8,128)(2,1)} %gather_fusion.2), calls=%async_computation.2 | async-start | bytes 4194304 | tf_op jit(solution)/shard_map/all_to_all | solution.py:65
  211.1 188.9 %all-to-all-start.7 = ((bf16[32,128,250]{2,1,0:T(8,128)(2,1)}), bf16[32,128,250]{2,1,0:T(8,128)(2,1)}, u32[]{:S(2)}, u32[]{:S(2)}) async-start(bf16[32,128,250]{2,1,0:T(8,128)(2,1)} %gather_fusion.12), calls=%async_computation.7 | async-start | bytes 4194304 | tf_op jit(solution)/shard_map/all_to_all | solution.py:65
  219.5 105.3 %all-reduce.5.cloned.1.call-start = ((), (), s32[]{:S(2)}) async-start(), calls=%async_computation.15 | async-start | bytes 786432 | tf_op jit(solution)/shard_map/psum | solution.py:71
  219.6 31.1 %copy-start.4 = (pred[6,128,256]{1,2,0:T(32,128)(4,1)S(1)}, pred[6,128,256]{1,2,0:T(32,128)(4,1)}, u32[]{:S(2)}) copy-start(pred[6,128,256]{1,2,0:T(32,128)(4,1)} %copy.177) | copy-start | bytes 589828
  252.2 146.8 %all-reduce.7.cloned.1.call-start = ((), (), s32[]{:S(2)}) async-start(), calls=%async_computation.16 | async-start | bytes 786432 | tf_op jit(solution)/shard_map/psum | solution.py:71
  325.8 147.4 %all-reduce.9.cloned.1.call-start = ((), (), s32[]{:S(2)}) async-start(), calls=%async_computation.17 | async-start | bytes 786432 | tf_op jit(solution)/shard_map/psum | solution.py:71
  400.0 147.2 %all-reduce.11.cloned.1.call-start = ((), (), s32[]{:S(2)}) async-start(), calls=%async_computation.18 | async-start | bytes 786432 | tf_op jit(solution)/shard_map/psum | solution.py:71
  553.2 34.0 %all-to-all-start.6 = ((bf16[32,128,250]{2,1,0:T(8,128)(2,1)}), bf16[32,128,250]{2,1,0:T(8,128)(2,1)}, u32[]{:S(2)}, u32[]{:S(2)}) async-start(bf16[32,128,250]{2,1,0:T(8,128)(2,1)} %gather_fusion.10), calls=%async_computation.6 | async-start | bytes 4194304 | tf_op jit(solution)/shard_map/all_to_all | solution.py:79
  587.2 34.8 %all-to-all-start.5 = ((bf16[32,128,250]{2,1,0:T(8,128)(2,1)}), bf16[32,128,250]{2,1,0:T(8,128)(2,1)}, u32[]{:S(2)}, u32[]{:S(2)}) async-start(bf16[32,128,250]{2,1,0:T(8,128)(2,1)} %gather_fusion.8), calls=%async_computation.5 | async-start | bytes 4194304 | tf_op jit(solution)/shard_map/all_to_all | solution.py:79
  622.0 34.8 %all-to-all-start.8 = ((bf16[32,128,250]{2,1,0:T(8,128)(2,1)}), bf16[32,128,250]{2,1,0:T(8,128)(2,1)}, u32[]{:S(2)}, u32[]{:S(2)}) async-start(bf16[32,128,250]{2,1,0:T(8,128)(2,1)} %gather_fusion.14), calls=%async_computation.8 | async-start | bytes 4194304 | tf_op jit(solution)/shard_map/all_to_all | solution.py:79
  630.4 39.4 %reduce-scatter.13.cloned.1.call-start = ((), (), s32[]{:S(2)}) async-start(), calls=%async_computation.19 | async-start | bytes 442368
  656.9 52.5 %all-to-all-start.9 = ((bf16[32,128,250]{2,1,0:T(8,128)(2,1)}), bf16[32,128,250]{2,1,0:T(8,128)(2,1)}, u32[]{:S(2)}, u32[]{:S(2)}) async-start(bf16[32,128,250]{2,1,0:T(8,128)(2,1)} %gather_fusion.16), calls=%async_computation.9 | async-start | bytes 4194304 | tf_op jit(solution)/shard_map/all_to_all | solution.py:79
  665.2 43.1 %reduce-scatter.15.cloned.1.call-start = ((), (), s32[]{:S(2)}) async-start(), calls=%async_computation.20 | async-start | bytes 442368
  670.8 76.3 %reduce-scatter.17.cloned.1.call-start = ((), (), s32[]{:S(2)}) async-start(), calls=%async_computation.21 | async-start | bytes 442368
  709.3 76.3 %reduce-scatter.19.cloned.1.call-start = ((), (), s32[]{:S(2)}) async-start(), calls=%async_computation.22 | async-start | bytes 442368
  711.6 90.1 %copy-start.1 = (bf16[768,768]{1,0:T(8,128)(2,1)S(1)}, bf16[768,768]{1,0:T(8,128)(2,1)}, u32[]{:S(2)}) copy-start(bf16[768,768]{1,0:T(8,128)(2,1)} %param.5) | copy-start | bytes 3538948
  (3 other events, 52.7 us)
Sparse Core Ops, SparseCore 0:
  252.3 72.5 all-reduce.4
  327.2 71.7 all-reduce.6
  401.3 71.8 all-reduce.8
  475.4 71.8 all-reduce.10
  633.8 35.9 reduce-scatter.12
  672.2 36.1 reduce-scatter.14
  710.9 36.1 reduce-scatter.16
  749.5 36.0 reduce-scatter.18
where the time goes:
time: 810 us; the launch traced here: 809 us
  waiting for transfers between devices  584 us (72%)
  starting transfers between devices  81.6 us (10%)
  local copies, waits for them, and re-layouts  61.3 us (8%)
  blocking collectives  42.4 us (5%)
  other arithmetic  17.1 us (2%)
  between operations  13.9 us (2%)
    psum x4, waiting for transfers between devices, body(): sums.append(lax.psum(partial_one, 'row'))  284 us
    unnamed x12, waiting for transfers between devices  105 us
    all_to_all x1, waiting for transfers between devices, body(): lax.all_to_all(send_emb, 'col', split_axis=0, concat_axis=0, tiled=True)  70.4 us
    all_to_all x4, waiting for transfers between devices, body(): lax.all_to_all(send_spread, 'col', split_axis=0, concat_axis=0, tiled=True)  69.5 us
    all_to_all x4, waiting for transfers between devices, body(): lax.all_to_all(send_lab, 'col', split_axis=0, concat_axis=0, tiled=True)  54 us
    all_to_all x4, starting transfers between devices, body(): lax.all_to_all(send_spread, 'col', split_axis=0, concat_axis=0, tiled=True)  32.6 us
    all_to_all x4, starting transfers between devices, body(): lax.all_to_all(send_lab, 'col', split_axis=0, concat_axis=0, tiled=True)  32.5 us
    all_gather x1, blocking collectives, body(): stats = lax.all_gather(jnp.stack([local_max, local_sum]), 'row')  28.4 us
  transfers between devices with their start and end apart: 18, of which 16 were waited for; matrix products, arithmetic and copies ran while one was open for 9% of the time, Pallas kernels for 0%

commit v1 on v0

--- a/solution.py
+++ b/solution.py
@@ -68,7 +68,7 @@
         partial_one = propagate_using(weight_matrix, fetched[k]).astype(jnp.bfloat16)
         if k > 0:
             partial_one, sums[k - 1] = lax.optimization_barrier((partial_one, sums[k - 1]))
-        sums.append(lax.psum(partial_one, "row"))
+        sums.append(jnp.sum(lax.all_gather(partial_one, axis_name="row"), 0))
     spreads = []
     for k in range(CHUNKS):
         summed = sums[k].astype(jnp.float32)

time: 810 us -> 583 us (0.72)
  waiting for transfers between devices: 584 us -> 274 us
  blocking collectives: 42.4 us -> 146 us
  starting transfers between devices: 81.6 us -> 56.1 us
    psum x4 -> x0, waiting for transfers between devices: 284 us -> none  [body(): sums.append(lax.psum(partial_one, 'row'))]
    all_to_all x0 -> x3, blocking collectives: none -> 104 us  [body(): lax.all_to_all(send_lab, 'col', split_axis=0, concat_axis=0, tiled=True)]
    reduce_scatter x0 -> x1, waiting for transfers between devices: none -> 35.8 us  [body(): lax.psum_scatter(partial_two, 'row', scatter_dimension=0, tiled=True)]
    all_to_all x4 -> x1, waiting for transfers between devices: 54 us -> 22.8 us  [body(): lax.all_to_all(send_lab, 'col', split_axis=0, concat_axis=0, tiled=True)]
    unnamed x12 -> x11, waiting for transfers between devices: 105 us -> 74 us
    all_to_all x4 -> x1, starting transfers between devices: 32.5 us -> 7.11 us  [body(): lax.all_to_all(send_lab, 'col', split_axis=0, concat_axis=0, tiled=True)]
    all_gather x0 -> x4, waiting for transfers between devices: none -> 12 us  [body(): sums.append(jnp.sum(lax.all_gather(partial_one, axis_name='row'), 0))]
    reduce_sum x0 -> x4, other arithmetic: none -> 11.8 us  [body(): sums.append(jnp.sum(lax.all_gather(partial_one, axis_name='row'), 0))]
  transfers between devices with their start and end apart: 18 -> 15, of which waited for: 16 -> 13; matrix products, arithmetic and copies ran while one was open for 9% -> 10% of each run, Pallas kernels for 0% -> 0%
where the time goes in v1:
time: 583 us; the launch traced here: 581 us
  waiting for transfers between devices  274 us (47%)
  blocking collectives  146 us (25%)
  starting transfers between devices  56.1 us (10%)
  local copies, waits for them, and re-layouts  54.1 us (9%)
  other arithmetic  24.2 us (4%)
  between operations  13.9 us (2%)
  matrix products  12.2 us (2%)
    all_to_all x3, blocking collectives, body(): lax.all_to_all(send_lab, 'col', split_axis=0, concat_axis=0, tiled=True)  104 us
    unnamed x11, waiting for transfers between devices  74 us
    all_to_all x4, waiting for transfers between devices, body(): lax.all_to_all(send_spread, 'col', split_axis=0, concat_axis=0, tiled=True)  66.6 us
    all_to_all x1, waiting for transfers between devices, body(): lax.all_to_all(send_emb, 'col', split_axis=0, concat_axis=0, tiled=True)  62.8 us
    reduce_scatter x1, waiting for transfers between devices, body(): lax.psum_scatter(partial_two, 'row', scatter_dimension=0, tiled=True)  35.8 us
    all_to_all x4, starting transfers between devices, body(): lax.all_to_all(send_spread, 'col', split_axis=0, concat_axis=0, tiled=True)  32.7 us
    all_gather x1, blocking collectives, body(): stats = lax.all_gather(jnp.stack([local_max, local_sum]), 'row')  28.3 us
    all_to_all x1, waiting for transfers between devices, body(): lax.all_to_all(send_lab, 'col', split_axis=0, concat_axis=0, tiled=True)  22.8 us
  transfers between devices with their start and end apart: 15, of which 13 were waited for; matrix products, arithmetic and copies ran while one was open for 10% of the time, Pallas kernels for 0%

profile of v1, /device:TPU:4, one launch (start us, length us, event | category | flops | bytes accessed | tf_op | source)
XLA Modules:
  0.0 580.8 jit_solution(7901876910142957053)
XLA Ops:
  8.2 7.6 %all-to-all-start = ((s32[32,1,1]{2,1,0:T(1,128)}), s32[32,1,1]{2,1,0:T(1,128)S(1)}, u32[]{:S(2)}, u32[]{:S(2)}) async-start(s32[32,1,1]{2,1,0:T(1,128)} %copy.145), calls=%async_computation | async-start | bytes 32768 | tf_op jit(solution)/shard_map/all_to_all | solution.py:28
  23.7 7.1 %all-to-all-start.4 = ((bf16[32,128,250]{2,1,0:T(8,128)(2,1)}), bf16[32,128,250]{2,1,0:T(8,128)(2,1)}, u32[]{:S(2)}, u32[]{:S(2)}) async-start(bf16[32,128,250]{2,1,0:T(8,128)(2,1)} %gather_fusion.6), calls=%async_computation.4 | async-start | bytes 4194304 | tf_op jit(solution)/shard_map/all_to_all | solution.py:65
  34.4 22.8 %all-to-all-done.4 = bf16[32,128,250]{2,1,0:T(8,128)(2,1)} async-done(((bf16[32,128,250]{2,1,0:T(8,128)(2,1)}), bf16[32,128,250]{2,1,0:T(8,128)(2,1)}, u32[]{:S(2)}, u32[]{:S(2)}) %all-to-all-start.4) | async-done | bytes 2048032 | tf_op jit(solution)/shard_map/all_to_all | solution.py:65
  57.2 8.5 %all-to-all-start.1 = ((bf16[32,128,768]{2,1,0:T(8,128)(2,1)}), bf16[32,128,768]{2,1,0:T(8,128)(2,1)}, u32[]{:S(2)}, u32[]{:S(2)}) async-start(bf16[32,128,768]{2,1,0:T(8,128)(2,1)} %gather_fusion), calls=%async_computation.1 | async-start | bytes 12582912 | tf_op jit(solution)/shard_map/all_to_all | solution.py:45
  65.8 7.2 %fusion = pred[768,256]{1,0:T(8,128)(4,1)S(1)} fusion(s32[768,50]{0,1:T(8,128)S(1)} %and_select_fusion), kind=kLoop, calls=%fused_computation.19 | loop fusion | flops 19464192 | bytes 350208 | tf_op jit(solution)/shard_map/reduce_or | solution.py:34
  76.4 62.8 %all-to-all-done.1 = bf16[32,128,768]{2,1,0:T(8,128)(2,1)} async-done(((bf16[32,128,768]{2,1,0:T(8,128)(2,1)}), bf16[32,128,768]{2,1,0:T(8,128)(2,1)}, u32[]{:S(2)}, u32[]{:S(2)}) %all-to-all-start.1) | async-done | bytes 6291488 | tf_op jit(solution)/shard_map/all_to_all | solution.py:45
  139.2 5.0 gather_fusion.1
  146.9 28.3 %all-gather = f32[16,6,128]{2,1,0:T(8,128)S(1)} all-gather(f32[2,6,128]{2,1,0:T(8,128)S(1)} %pad_maximum_fusion.1), channel_id=2, replica_groups=mesh['row'=8,'col'=32] {'row'}, dimensions={0}, use_global_device_ids=true | all-gather | bytes 55296 | tf_op jit(solution)/shard_map/all_gather | solution.py:53
  178.6 35.7 %all_to_all.76 = bf16[32,128,250]{2,1,0:T(8,128)(2,1)} all-to-all(bf16[32,128,250]{2,1,0:T(8,128)(2,1)} %gather_fusion.4), channel_id=1, replica_groups=mesh['row'=8,'col'=32] {'col'}, dimensions={0} | all-to-all | bytes 4096000 | tf_op jit(solution)/shard_map/all_to_all | solution.py:65
  225.5 34.0 %all_to_all.77 = bf16[32,128,250]{2,1,0:T(8,128)(2,1)} all-to-all(bf16[32,128,250]{2,1,0:T(8,128)(2,1)} %gather_fusion.2), channel_id=1, replica_groups=mesh['row'=8,'col'=32] {'col'}, dimensions={0} | all-to-all | bytes 4096000 | tf_op jit(solution)/shard_map/all_to_all | solution.py:65
  262.8 4.4 all-gather.11.cloned.1.call-done
  272.5 34.0 %all_to_all.78 = bf16[32,128,250]{2,1,0:T(8,128)(2,1)} all-to-all(bf16[32,128,250]{2,1,0:T(8,128)(2,1)} %gather_fusion.12), channel_id=1, replica_groups=mesh['row'=8,'col'=32] {'col'}, dimensions={0} | all-to-all | bytes 4096000 | tf_op jit(solution)/shard_map/all_to_all | solution.py:65
  309.8 4.4 all-gather.13.cloned.1.call-done
  321.5 7.6 %all-to-all-start.6 = ((bf16[32,128,250]{2,1,0:T(8,128)(2,1)}), bf16[32,128,250]{2,1,0:T(8,128)(2,1)}, u32[]{:S(2)}, u32[]{:S(2)}) async-start(bf16[32,128,250]{2,1,0:T(8,128)(2,1)} %gather_fusion.10), calls=%async_computation.6 | async-start | bytes 4194304 | tf_op jit(solution)/shard_map/all_to_all | solution.py:79
  331.8 23.8 %all-to-all-done.6 = bf16[32,128,250]{2,1,0:T(8,128)(2,1)} async-done(((bf16[32,128,250]{2,1,0:T(8,128)(2,1)}), bf16[32,128,250]{2,1,0:T(8,128)(2,1)}, u32[]{:S(2)}, u32[]{:S(2)}) %all-to-all-start.6) | async-done | bytes 2048032 | tf_op jit(solution)/shard_map/all_to_all | solution.py:79
  355.5 8.3 %all-to-all-start.5 = ((bf16[32,128,250]{2,1,0:T(8,128)(2,1)}), bf16[32,128,250]{2,1,0:T(8,128)(2,1)}, u32[]{:S(2)}, u32[]{:S(2)}) async-start(bf16[32,128,250]{2,1,0:T(8,128)(2,1)} %gather_fusion.8), calls=%async_computation.5 | async-start | bytes 4194304 | tf_op jit(solution)/shard_map/all_to_all | solution.py:79
  365.9 24.5 %all-to-all-done.5 = bf16[32,128,250]{2,1,0:T(8,128)(2,1)} async-done(((bf16[32,128,250]{2,1,0:T(8,128)(2,1)}), bf16[32,128,250]{2,1,0:T(8,128)(2,1)}, u32[]{:S(2)}, u32[]{:S(2)}) %all-to-all-start.5) | async-done | bytes 2048032 | tf_op jit(solution)/shard_map/all_to_all | solution.py:79
  390.4 8.3 %all-to-all-start.8 = ((bf16[32,128,250]{2,1,0:T(8,128)(2,1)}), bf16[32,128,250]{2,1,0:T(8,128)(2,1)}, u32[]{:S(2)}, u32[]{:S(2)}) async-start(bf16[32,128,250]{2,1,0:T(8,128)(2,1)} %gather_fusion.14), calls=%async_computation.8 | async-start | bytes 4194304 | tf_op jit(solution)/shard_map/all_to_all | solution.py:79
  406.9 18.3 %all-to-all-done.8 = bf16[32,128,250]{2,1,0:T(8,128)(2,1)} async-done(((bf16[32,128,250]{2,1,0:T(8,128)(2,1)}), bf16[32,128,250]{2,1,0:T(8,128)(2,1)}, u32[]{:S(2)}, u32[]{:S(2)}) %all-to-all-start.8) | async-done | bytes 2048032 | tf_op jit(solution)/shard_map/all_to_all | solution.py:79
  425.2 8.3 %all-to-all-start.9 = ((bf16[32,128,250]{2,1,0:T(8,128)(2,1)}), bf16[32,128,250]{2,1,0:T(8,128)(2,1)}, u32[]{:S(2)}, u32[]{:S(2)}) async-start(bf16[32,128,250]{2,1,0:T(8,128)(2,1)} %gather_fusion.16), calls=%async_computation.9 | async-start | bytes 4194304 | tf_op jit(solution)/shard_map/all_to_all | solution.py:79
  442.5 34.3 %reduce-scatter.15.cloned.1.call-done = bf16[96,250]{1,0:T(8,128)(2,1)} async-done(((bf16[768,250]{1,0:T(8,128)(2,1)}), bf16[96,250]{1,0:T(8,128)(2,1)}) %reduce-scatter.15.cloned.1.call-update) | async-done | bytes 48016
  477.8 37.6 %reduce-scatter.17.cloned.1.call-done = bf16[96,250]{1,0:T(8,128)(2,1)} async-done(((bf16[768,250]{1,0:T(8,128)(2,1)}), bf16[96,250]{1,0:T(8,128)(2,1)}) %reduce-scatter.17.cloned.1.call-update) | async-done | bytes 48016
  522.2 35.8 %reduce-scatter.19.cloned.1.call-done = bf16[96,250]{1,0:T(8,128)(2,1)} async-done(((bf16[768,250]{1,0:T(8,128)(2,1)}), bf16[96,250]{1,0:T(8,128)(2,1)}) %reduce-scatter.19.cloned.1.call-update) | async-done | bytes 48016 | tf_op jit(solution)/shard_map/reduce_scatter | solution.py:85
  559.3 14.0 %all_to_all.79 = bf16[96,8,125]{2,0,1:T(8,128)(2,1)S(1)} all-to-all(bf16[96,8,125]{2,0,1:T(8,128)(2,1)S(1)} %copy.167), channel_id=1, replica_groups=mesh['row'=8,'col'=32] {'row'}, dimensions={1} | all-to-all | bytes 384000 | tf_op jit(solution)/shard_map/all_to_all | solution.py:94
  (96 shorter events, 84.2 us)
Async XLA Ops:
  6.5 24.3 %copy-start = (bf16[768,768]{1,0:T(8,128)(2,1)S(1)}, bf16[768,768]{1,0:T(8,128)(2,1)}, u32[]{:S(2)}) copy-start(bf16[768,768]{1,0:T(8,128)(2,1)} %param.5) | copy-start | bytes 3538948
  8.2 12.8 %all-to-all-start = ((s32[32,1,1]{2,1,0:T(1,128)}), s32[32,1,1]{2,1,0:T(1,128)S(1)}, u32[]{:S(2)}, u32[]{:S(2)}) async-start(s32[32,1,1]{2,1,0:T(1,128)} %copy.145), calls=%async_computation | async-start | bytes 32768 | tf_op jit(solution)/shard_map/all_to_all | solution.py:28
  23.7 33.5 %all-to-all-start.4 = ((bf16[32,128,250]{2,1,0:T(8,128)(2,1)}), bf16[32,128,250]{2,1,0:T(8,128)(2,1)}, u32[]{:S(2)}, u32[]{:S(2)}) async-start(bf16[32,128,250]{2,1,0:T(8,128)(2,1)} %gather_fusion.6), calls=%async_computation.4 | async-start | bytes 4194304 | tf_op jit(solution)/shard_map/all_to_all | solution.py:65
  34.4 31.4 %copy-start.3 = (s32[768,50]{0,1:T(8,128)S(1)}, s32[768,50]{0,1:T(8,128)}, u32[]{:S(2)}) copy-start(s32[768,50]{0,1:T(8,128)} %param.9) | copy-start | bytes 460804
  34.4 38.9 %copy-start.4 = (f32[768]{0:T(1024)S(1)}, f32[768]{0:T(1024)}, u32[]{:S(2)}) copy-start(f32[768]{0:T(1024)} %param.7) | copy-start | bytes 9220
  57.2 82.0 %all-to-all-start.1 = ((bf16[32,128,768]{2,1,0:T(8,128)(2,1)}), bf16[32,128,768]{2,1,0:T(8,128)(2,1)}, u32[]{:S(2)}, u32[]{:S(2)}) async-start(bf16[32,128,768]{2,1,0:T(8,128)(2,1)} %gather_fusion), calls=%async_computation.1 | async-start | bytes 12582912 | tf_op jit(solution)/shard_map/all_to_all | solution.py:45
  65.6 155.1 %all-gather.9.cloned.1.call-start = ((), (), s32[]{:S(2)}) async-start(), calls=%async_computation.15 | async-start | bytes 3538944 | tf_op jit(solution)/shard_map/all_gather | solution.py:71
  146.6 28.8 %copy-start.2 = (bf16[12,128,250]{2,1,0:T(8,128)(2,1)S(1)}, bf16[12,128,250]{2,1,0:T(8,128)(2,1)}, u32[]{:S(2)}) copy-start(bf16[12,128,250]{2,1,0:T(8,128)(2,1)} %gather_fusion.7) | copy-start | bytes 2304004
  176.6 90.6 %all-gather.11.cloned.1.call-start = ((), (), s32[]{:S(2)}) async-start(), calls=%async_computation.16 | async-start | bytes 3538944 | tf_op jit(solution)/shard_map/all_gather | solution.py:71
  223.4 90.9 %all-gather.13.cloned.1.call-start = ((), (), s32[]{:S(2)}) async-start(), calls=%async_computation.17 | async-start | bytes 3538944 | tf_op jit(solution)/shard_map/all_gather | solution.py:71
  321.5 34.0 %all-to-all-start.6 = ((bf16[32,128,250]{2,1,0:T(8,128)(2,1)}), bf16[32,128,250]{2,1,0:T(8,128)(2,1)}, u32[]{:S(2)}, u32[]{:S(2)}) async-start(bf16[32,128,250]{2,1,0:T(8,128)(2,1)} %gather_fusion.10), calls=%async_computation.6 | async-start | bytes 4194304 | tf_op jit(solution)/shard_map/all_to_all | solution.py:79
  329.1 72.9 %all-gather.15.cloned.1.call-start = ((), (), s32[]{:S(2)}) async-start(), calls=%async_computation.18 | async-start | bytes 3538944 | tf_op jit(solution)/shard_map/all_gather | solution.py:71
  355.5 34.8 %all-to-all-start.5 = ((bf16[32,128,250]{2,1,0:T(8,128)(2,1)}), bf16[32,128,250]{2,1,0:T(8,128)(2,1)}, u32[]{:S(2)}, u32[]{:S(2)}) async-start(bf16[32,128,250]{2,1,0:T(8,128)(2,1)} %gather_fusion.8), calls=%async_computation.5 | async-start | bytes 4194304 | tf_op jit(solution)/shard_map/all_to_all | solution.py:79
  390.4 34.8 %all-to-all-start.8 = ((bf16[32,128,250]{2,1,0:T(8,128)(2,1)}), bf16[32,128,250]{2,1,0:T(8,128)(2,1)}, u32[]{:S(2)}, u32[]{:S(2)}) async-start(bf16[32,128,250]{2,1,0:T(8,128)(2,1)} %gather_fusion.14), calls=%async_computation.8 | async-start | bytes 4194304 | tf_op jit(solution)/shard_map/all_to_all | solution.py:79
  398.7 39.6 %reduce-scatter.13.cloned.1.call-start = ((), (), s32[]{:S(2)}) async-start(), calls=%async_computation.19 | async-start | bytes 442368
  425.2 91.1 %all-to-all-start.9 = ((bf16[32,128,250]{2,1,0:T(8,128)(2,1)}), bf16[32,128,250]{2,1,0:T(8,128)(2,1)}, u32[]{:S(2)}, u32[]{:S(2)}) async-start(bf16[32,128,250]{2,1,0:T(8,128)(2,1)} %gather_fusion.16), calls=%async_computation.9 | async-start | bytes 4194304 | tf_op jit(solution)/shard_map/all_to_all | solution.py:79
  433.5 43.2 %reduce-scatter.15.cloned.1.call-start = ((), (), s32[]{:S(2)}) async-start(), calls=%async_computation.20 | async-start | bytes 442368
  439.2 76.2 %reduce-scatter.17.cloned.1.call-start = ((), (), s32[]{:S(2)}) async-start(), calls=%async_computation.21 | async-start | bytes 442368
  477.7 80.3 %reduce-scatter.19.cloned.1.call-start = ((), (), s32[]{:S(2)}) async-start(), calls=%async_computation.22 | async-start | bytes 442368 | tf_op jit(solution)/shard_map/reduce_scatter | solution.py:85
  519.5 54.5 %copy-start.1 = (bf16[768,768]{1,0:T(8,128)(2,1)S(1)}, bf16[768,768]{1,0:T(8,128)(2,1)}, u32[]{:S(2)}) copy-start(bf16[768,768]{1,0:T(8,128)(2,1)} %param.5) | copy-start | bytes 3538948
Sparse Core Ops, SparseCore 0:
  176.7 44.0 all-gather.8
  223.5 43.5 all-gather.10
  270.6 43.5 all-gather.12
  331.4 43.5 all-gather.14
  402.2 36.0 reduce-scatter.12
  440.6 36.1 reduce-scatter.14
  479.3 36.0 reduce-scatter.16
  521.9 36.0 reduce-scatter.18
